TPU v7x, 32 devices: a whole 2x2x4 slice. The times are simulated.
32 devices in a mesh: band: 16 (over z, x, core), chan: 2 (over y).
Axes of the slice: x: 2, y: 2, z: 4, core: 2. Of those that a mesh axis runs over, the one named last changes fastest.
Arguments:
- features: bfloat16 [256, 64, 1024], P('chan', 'band'), may hold values from -6 to 6
- depth_kernel: bfloat16 [3, 9, 256], P(None, None, 'chan'), may hold values from -2 to 2
- pointwise: bfloat16 [4, 256, 256], P(None, 'chan'), may hold values from -0.25 to 0.25
- cotangent: bfloat16 [256, 64, 1024], P('chan', 'band'), may hold values from -6 to 6
Outputs:
- output: bfloat16 [256, 64, 1024], P('chan', 'band')
- grad_input: float32 [256, 64, 1024], P('chan', 'band')
- grad_depth: float32 [3, 9, 256], P(None, None, 'chan')
- grad_point: float32 [4, 256, 256], P(None, 'chan')
All inputs are finite; a program needn't handle non-finite values.
Results may differ from a plain program's by a relative error of at most 0.0057.
Values may be sent and summed in bfloat16 or wider, within the bound.
No kernel may reach another device: no remote copies, remote signals or barrier semaphores. Data moves between devices by JAX's collectives and lax.ppermute only.
A program may use at most 128 MiB of HBM per device.

v0:
```python
import jax
import jax.numpy as jnp
from jax import lax
from jax.sharding import PartitionSpec as P

GSCALE = 1024


dilations = (6, 12, 18)


def shifted(block, axis, distance):
    devices = range(lax.axis_size(axis))
    route = [(i - distance, i) for i in devices if i - distance in devices]
    return lax.ppermute(block, axis, route)


def window(padded, margin, spacing, row_step, col_step, height):
    first = margin + row_step * spacing
    piece = padded[:, first : first + height, :]
    return jnp.roll(piece, -col_step * spacing, axis=-1)


def extend(field, margin):
    height = field.shape[1]
    reach = -(-margin // height)
    northern = []
    southern = []
    for distance in range(1, reach + 1):
        first = max(0, distance * height - margin)
        northern.insert(0, shifted(field[:, first:, :], "band", distance))
        taken = min(height, margin - (distance - 1) * height)
        southern.append(shifted(field[:, :taken, :], "band", -distance))
    return jnp.concatenate(northern + [field] + southern, axis=1)


def local(features, depth_kernel, pointwise, cotangent):
    height = features.shape[1]
    kernel = depth_kernel.astype(jnp.float32)
    feat_wide = extend(features, 18)
    branches = [features]
    for which, spacing in enumerate(dilations):
        total = jnp.zeros(features.shape, jnp.float32)
        for tap_index in range(9):
            row_step = tap_index // 3 - 1
            col_step = tap_index % 3 - 1
            total = total + kernel[which, tap_index][:, None, None] * window(
                feat_wide, 18, spacing, row_step, col_step, height
            )
        branches.append(total.astype(jnp.bfloat16))
    stacked = jnp.stack(branches)
    output = lax.psum_scatter(
        jnp.einsum("bchw,bco->ohw", stacked, pointwise, preferred_element_type=jnp.float32).astype(
            jnp.bfloat16
        ),
        "chan",
        scatter_dimension=0,
        tiled=True,
    )
    cot_full = lax.all_gather(cotangent, "chan", axis=0, tiled=True)
    grad_sum = jnp.einsum("bco,ohw->bchw", pointwise, cot_full, preferred_element_type=jnp.float32)
    point_local = jnp.einsum("bchw,ohw->bco", stacked, cot_full, preferred_element_type=jnp.float32)
    grad_branches = grad_sum.astype(jnp.bfloat16)
    grad_input = grad_branches[0].astype(jnp.float32)
    depth_rows = []
    for which, spacing in enumerate(dilations):
        grad_field = grad_branches[which + 1]
        grad_f = grad_field.astype(jnp.float32)
        grad_wide = extend(grad_field, spacing)
        tap_rows = []
        for tap_index in range(9):
            row_step = tap_index // 3 - 1
            col_step = tap_index % 3 - 1
            grad_input = grad_input + kernel[which, tap_index][:, None, None] * window(
                grad_wide, spacing, spacing, -row_step, -col_step, height
            )
            tap_rows.append(
                jnp.sum(
                    grad_f * window(feat_wide, 18, spacing, row_step, col_step, height), axis=(1, 2)
                )
            )
        depth_rows.append(jnp.stack(tap_rows))
    depth_local = jnp.stack(depth_rows)
    depth_total, point_total = lax.psum((depth_local, point_local), "band")
    return (output, grad_input, depth_total / GSCALE, point_total / GSCALE)


def solution(mesh):
    return jax.shard_map(
        local,
        mesh=mesh,
        in_specs=(
            P("chan", "band", None),
            P(None, None, "chan"),
            P(None, "chan", None),
            P("chan", "band", None),
        ),
        out_specs=(
            P("chan", "band", None),
            P("chan", "band", None),
            P(None, None, "chan"),
            P(None, "chan", None),
        ),
        check_vma=False,
    )
```

profile of v0, /device:TPU:3, one launch (start us, length us, event | category | flops | bytes accessed | tf_op | source)
XLA Modules:
  0.0 359.1 jit_solution(2100974339462868979)
XLA Ops:
  7.2 2.0 copy.40
  10.6 2.6 collective-permute-start.2
  13.2 3.8 %collective-permute-start = (bf16[128,4,1024]{0,2,1:T(8,128)(2,1)S(1)}, bf16[128,4,1024]{0,2,1:T(8,128)(2,1)}, u32[]{:S(2)}, u32[]{:S(2)}) collective-permute-start(bf16[128,4,1024]{0,2,1:T(8,128)(2,1)S(1)} %copy.40), channel_id=1, source_target_pairs={{0,4},{2,6},{4,8},{6,10},{8,12},{10,14},{12,16},{14,18},{16,20},{1... | collective-permute-start | bytes 3145736 | tf_op jit(solution)/shard_map/ppermute | solution.py:15
  18.4 4.8 %collective-permute-start.6 = (bf16[128,2,1024]{0,2,1:T(8,128)(2,1)S(1)}, bf16[128,2,1024]{0,2,1:T(8,128)(2,1)S(1)}, u32[]{:S(2)}, u32[]{:S(2)}) collective-permute-start(bf16[128,2,1024]{0,2,1:T(8,128)(2,1)S(1)} %get-tuple-element.118), channel_id=1, source_target_pairs={{0,10},{2,12},{4,14},{6,16},{8,18},{10,20},{12,22},{14,24},{16,26}... | collective-permute-start | bytes 1572872 | tf_op jit(solution)/shard_map/ppermute | solution.py:15
  27.3 24.4 %collective-permute-done.6 = bf16[128,2,1024]{0,2,1:T(8,128)(2,1)S(1)} collective-permute-done((bf16[128,2,1024]{0,2,1:T(8,128)(2,1)S(1)}, bf16[128,2,1024]{0,2,1:T(8,128)(2,1)S(1)}, u32[]{:S(2)}, u32[]{:S(2)}) %collective-permute-start.6) | collective-permute-done | bytes 524320 | tf_op jit(solution)/shard_map/ppermute | solution.py:15
  51.7 13.5 %collective-permute-start.7 = (bf16[128,4,1024]{0,2,1:T(8,128)(2,1)S(1)}, bf16[128,4,1024]{0,2,1:T(8,128)(2,1)S(1)}, u32[]{:S(2)}, u32[]{:S(2)}) collective-permute-start(bf16[128,4,1024]{0,2,1:T(8,128)(2,1)S(1)} %copy.40), channel_id=1, source_target_pairs={{0,8},{2,10},{4,12},{6,14},{8,16},{10,18},{12,20},{14,22},{16,24},... | collective-permute-start | bytes 3145736 | tf_op jit(solution)/shard_map/ppermute | solution.py:15
  65.2 3.1 collective-permute-start.4
  70.0 1.9 collective-permute-start.3
  73.3 1.9 collective-permute-start.5
  76.5 5.2 %collective-permute-start.1 = (bf16[128,4,1024]{0,2,1:T(8,128)(2,1)S(1)}, bf16[128,4,1024]{0,2,1:T(8,128)(2,1)S(1)}, u32[]{:S(2)}, u32[]{:S(2)}) collective-permute-start(bf16[128,4,1024]{0,2,1:T(8,128)(2,1)S(1)} %copy.40), channel_id=1, source_target_pairs={{0,2},{2,4},{4,6},{6,8},{8,10},{10,12},{12,14},{14,16},{16,18},{18... | collective-permute-start | bytes 3145736 | tf_op jit(solution)/shard_map/ppermute | solution.py:15
  83.0 3.3 collective-permute-done.7
  86.4 32.6 %collective-permute-done.4 = bf16[128,4,1024]{0,2,1:T(8,128)(2,1)S(1)} collective-permute-done((bf16[128,4,1024]{0,2,1:T(8,128)(2,1)S(1)}, bf16[128,4,1024]{0,2,1:T(8,128)(2,1)S(1)}, u32[]{:S(2)}, u32[]{:S(2)}) %collective-permute-start.4) | collective-permute-done | bytes 1048608 | tf_op jit(solution)/shard_map/ppermute | solution.py:15
  120.1 1.7 collective-permute-done.1
  124.8 4.1 %fusion.87 = bf16[1,128,4,1024]{1,3,0,2:T(8,128)(2,1)} fusion(f32[128]{0:T(128)} %get-tuple-element.130, bf16[128,4,1024]{0,2,1:T(8,128)(2,1)S(1)} %collective-permute-done.5, f32[128]{0:T(128)} %get-tuple-element.131, f32[128]{0:T(128)} %get-tuple-element.132, f32[128]{0:T(128)} %get-tuple-element.133, bf16[128,4,1024]{0,2,1:T(8,128)(2,1)S(1)} %copy.40, ...), kind=kLoop, calls=%fused_computation.168 | loop fusion | flops 23592960 | bytes 10490368 | tf_op jit(solution)/shard_map/stack | solution.py:51
  129.1 4.0 %fusion.86 = bf16[1,128,4,1024]{1,3,0,2:T(8,128)(2,1)} fusion(f32[128]{0:T(128)S(1)} %get-tuple-element.121, f32[128]{0:T(128)S(1)} %get-tuple-element.122, f32[128]{0:T(128)S(1)} %get-tuple-element.123, f32[128]{0:T(128)S(1)} %get-tuple-element.124, bf16[128,4,1024]{0,2,1:T(8,128)(2,1)S(1)} %copy.40, f32[128]{0:T(128)S(1)} %get-tuple-element.125, ...), kind=kLoop, calls=%fused_computation.167 | loop fusion | flops 23592960 | bytes 10490368 | tf_op jit(solution)/shard_map/stack | solution.py:51
  133.2 4.1 %fusion.88 = bf16[1,128,4,1024]{1,3,0,2:T(8,128)(2,1)} fusion(f32[128]{0:T(128)} %get-tuple-element.140, f32[128]{0:T(128)} %get-tuple-element.141, f32[128]{0:T(128)} %get-tuple-element.142, f32[128]{0:T(128)} %get-tuple-element.143, bf16[128,4,1024]{0,2,1:T(8,128)(2,1)S(1)} %copy.40, f32[128]{0:T(128)} %get-tuple-element.144, f32[128]{0:T(128)} %get-tuple-element.145, ...), kind=kLoop, calls=%fused_computation.169 | loop fusion | flops 23592960 | bytes 10490368 | tf_op jit(solution)/shard_map/stack | solution.py:51
  137.2 4.7 %fusion.83 = f32[4,128,256]{2,1,0:T(8,128)} fusion(bf16[256,4,1024]{2,0,1:T(8,128)(2,1)} %all-gather.2.cloned.1.call-done, bf16[1,128,4,1024]{1,3,0,2:T(8,128)(2,1)} %fusion.86, bf16[1,128,4,1024]{1,3,0,2:T(8,128)(2,1)} %fusion.87, bf16[1,128,4,1024]{1,3,0,2:T(8,128)(2,1)} %fusion.88, bf16[1,128,4,1024]{1,3,0,2:T(8,128)(2,1)S(1)} %bitcast.192), kind=kOutput, calls=%fused_computation.144 | convolution fusion | flops 1080033280 | bytes 6815744 | tf_op jit(solution)/shard_map/bchw,ohw->bco/dot_general | solution.py:62
  142.2 4.4 %bitcast_convert_fusion = bf16[4,1024,256]{2,1,0:T(8,128)(2,1)} fusion(bf16[1,128,4,1024]{1,3,0,2:T(8,128)(2,1)} %fusion.86, bf16[1,128,4,1024]{1,3,0,2:T(8,128)(2,1)} %fusion.87, bf16[1,128,4,1024]{1,3,0,2:T(8,128)(2,1)} %fusion.88, bf16[1,128,4,1024]{1,3,0,2:T(8,128)(2,1)S(1)} %bitcast.193, bf16[4,128,256]{2,1,0:T(8,128)(2,1)S(1)} %copy-done), kind=kOutput, calls=%fused_computation.34 | convolution fusion | flops 1081081856 | bytes 6553600 | tf_op jit(solution)/shard_map/bchw,bco->ohw/dot_general | solution.py:53
  146.6 4.1 %copy.79 = bf16[256,4096]{1,0:T(8,128)(2,1)} copy(bf16[256,4096]{0,1:T(8,128)(2,1)} %bitcast.195) | data formatting | bytes 4194304
  150.8 3.0 convolution_convert_fusion
  154.1 3.8 %fusion.58 = (f32[128]{0:T(128)S(1)}, f32[128]{0:T(128)S(1)}, f32[128]{0:T(128)S(1)}, f32[128]{0:T(128)S(1)}, f32[128]{0:T(128)S(1)}, /*index=5*/f32[128]{0:T(128)S(1)}, f32[128]{0:T(128)S(1)}) fusion(bf16[128,4,6]{0,2,1:T(8,128)(2,1)S(1)} %get-tuple-element.47, bf16[128,4,1018]{0,2,1:T(8,128)(2,1)S(1)} %copy-done.24, ...), kind=kLoop, calls=%fused_computation.118 | loop fusion | flops 19922048 | bytes 9440768 | tf_op jit(solution)/shard_map/reduce_sum | solution.py:78
  157.9 1.7 fusion.54
  162.0 12.7 %collective-permute-start.13 = (bf16[128,4,1024]{0,2,1:T(8,128)(2,1)S(1)}, bf16[128,4,1024]{0,2,1:T(8,128)(2,1)}, u32[]{:S(2)}, u32[]{:S(2)}) collective-permute-start(bf16[128,4,1024]{0,2,1:T(8,128)(2,1)S(1)} %get-tuple-element.39), channel_id=1, source_target_pairs={{0,2},{2,4},{4,6},{6,8},{8,10},{10,12},{12,14},{14,16},{16,18},{18... | collective-permute-start | bytes 3145736 | tf_op jit(solution)/shard_map/ppermute | solution.py:15
  174.8 1.9 collective-permute-start.10
  178.0 1.6 fusion.110
  179.7 1.7 fusion.114
  181.5 1.7 fusion.118
  183.2 2.9 collective-permute-start.12
  186.2 4.0 %fusion.57 = (f32[128]{0:T(128)S(1)}, f32[128]{0:T(128)S(1)}, f32[128]{0:T(128)S(1)}, f32[128]{0:T(128)S(1)}, f32[128]{0:T(128)S(1)}, /*index=5*/f32[128]{0:T(128)S(1)}, f32[128]{0:T(128)S(1)}) fusion(bf16[128,8,1024]{0,2,1:T(8,128)(2,1)S(1)} %copy-done.12, bf16[4,128,4,1024]{1,3,2,0:T(8,128)(2,1)S(1)} %convolution_convert_fusion, ...), kind=kLoop, calls=%fused_computation.117 | loop fusion | flops 20446336 | bytes 10489344 | tf_op jit(solution)/shard_map/reduce_sum | solution.py:78
  190.3 4.5 %fusion.56 = (f32[128]{0:T(128)S(1)}, f32[128]{0:T(128)S(1)}, f32[128]{0:T(128)S(1)}, f32[128]{0:T(128)S(1)}, f32[128]{0:T(128)S(1)}, /*index=5*/f32[128]{0:T(128)S(1)}, f32[128]{0:T(128)S(1)}) fusion(bf16[128,4,1018]{0,2,1:T(8,128)(2,1)} %copy-done.18, bf16[128,4,6]{0,2,1:T(8,128)(2,1)S(1)} %copy-done.65, bf16[4,128,4,1024]{1,3,2,0:T(8,128)(2,1)} %copy-done.2, ...), kind=kLoop, calls=%fused_computation.116 | loop fusion | flops 19922048 | bytes 9440768 | tf_op jit(solution)/shard_map/reduce_sum | solution.py:78
  194.9 57.9 %psum.14 = f32[3,9,128]{2,1,0:T(8,128)S(1)} all-reduce(f32[3,9,128]{2,1,0:T(8,128)S(1)} %pad_maximum_fusion.21), channel_id=1, replica_groups=mesh['band'=16,'chan'=2] {'band'}, use_global_device_ids=true, to_apply=%region_28.29 | all-reduce | flops 3456 | bytes 27648 | tf_op jit(solution)/shard_map/psum | solution.py:84
  253.3 5.7 %collective-permute-start.18 = (bf16[128,2,1024]{0,2,1:T(8,128)(2,1)}, bf16[128,2,1024]{0,2,1:T(8,128)(2,1)}, u32[]{:S(2)}, u32[]{:S(2)}) collective-permute-start(bf16[128,2,1024]{0,2,1:T(8,128)(2,1)} %get-tuple-element.97), channel_id=1, source_target_pairs={{0,10},{2,12},{4,14},{6,16},{8,18},{10,20},{12,22},{14,24},{16,26}... | collective-permute-start | bytes 1572872 | tf_op jit(solution)/shard_map/ppermute | solution.py:15
  259.1 1.9 broadcast_multiply_fusion
  261.0 2.9 collective-permute-start.11
  265.0 3.8 %collective-permute-done.18 = bf16[128,2,1024]{0,2,1:T(8,128)(2,1)} collective-permute-done((bf16[128,2,1024]{0,2,1:T(8,128)(2,1)}, bf16[128,2,1024]{0,2,1:T(8,128)(2,1)}, u32[]{:S(2)}, u32[]{:S(2)}) %collective-permute-start.18) | collective-permute-done | bytes 524320 | tf_op jit(solution)/shard_map/ppermute | solution.py:15
  268.8 6.9 %collective-permute-start.19 = (bf16[128,4,1024]{0,2,1:T(8,128)(2,1)S(1)}, bf16[128,4,1024]{0,2,1:T(8,128)(2,1)S(1)}, u32[]{:S(2)}, u32[]{:S(2)}) collective-permute-start(bf16[128,4,1024]{0,2,1:T(8,128)(2,1)S(1)} %get-tuple-element.40), channel_id=1, source_target_pairs={{0,8},{2,10},{4,12},{6,14},{8,16},{10,18},{12,20},{14,22},{16,24},... | collective-permute-start | bytes 3145736 | tf_op jit(solution)/shard_map/ppermute | solution.py:15
  276.9 2.1 collective-permute-start.15
  280.3 3.7 %collective-permute-start.14 = (bf16[128,4,1024]{0,2,1:T(8,128)(2,1)S(1)}, bf16[128,4,1024]{0,2,1:T(8,128)(2,1)S(1)}, u32[]{:S(2)}, u32[]{:S(2)}) collective-permute-start(bf16[128,4,1024]{0,2,1:T(8,128)(2,1)S(1)} %copy-done.14), channel_id=1, source_target_pairs={{6,0},{8,2},{10,4},{12,6},{14,8},{16,10},{18,12},{20,14},{22,16},{... | collective-permute-start | bytes 3145736 | tf_op jit(solution)/shard_map/ppermute | solution.py:15
  285.3 1.6 collective-permute-start.17
  286.9 1.4 constant_dynamic-update-slice_fusion.10
  288.3 10.3 %collective-permute-done.19 = bf16[128,4,1024]{0,2,1:T(8,128)(2,1)S(1)} collective-permute-done((bf16[128,4,1024]{0,2,1:T(8,128)(2,1)S(1)}, bf16[128,4,1024]{0,2,1:T(8,128)(2,1)S(1)}, u32[]{:S(2)}, u32[]{:S(2)}) %collective-permute-start.19) | collective-permute-done | bytes 1048608 | tf_op jit(solution)/shard_map/ppermute | solution.py:15
  298.8 20.9 %collective-permute-done.15 = bf16[128,4,1024]{0,2,1:T(8,128)(2,1)S(1)} collective-permute-done((bf16[128,4,1024]{0,2,1:T(8,128)(2,1)S(1)}, bf16[128,4,1024]{0,2,1:T(8,128)(2,1)S(1)}, u32[]{:S(2)}, u32[]{:S(2)}) %collective-permute-start.15) | collective-permute-done | bytes 1048608 | tf_op jit(solution)/shard_map/ppermute | solution.py:15
  319.7 6.4 %collective-permute-done.17 = bf16[128,2,1024]{0,2,1:T(8,128)(2,1)S(1)} collective-permute-done((bf16[128,2,1024]{0,2,1:T(8,128)(2,1)S(1)}, bf16[128,2,1024]{0,2,1:T(8,128)(2,1)S(1)}, u32[]{:S(2)}, u32[]{:S(2)}) %collective-permute-start.17) | collective-permute-done | bytes 524320 | tf_op jit(solution)/shard_map/ppermute | solution.py:15
  330.4 1.4 copy-done.3
  331.9 15.4 %fusion.49 = f32[128,4,1024]{0,2,1:T(8,128)S(1)} fusion(bf16[128,4,1024]{0,2,1:T(8,128)(2,1)S(1)} %collective-permute-done.15, bf16[128,4,1024]{0,2,1:T(8,128)(2,1)S(1)} %collective-permute-done.14, bf16[128,6,1024]{0,2,1:T(8,128)(2,1)S(1)} %constant_dynamic-update-slice_fusion.14, bf16[128,6,1024]{0,2,1:T(8,128)(2,1)S(1)} %constant_dynamic-update-slice_fusion.12, ...), kind=kLoop, calls=%fused_computation.109 | loop fusion | flops 71303168 | bytes 31471104 | tf_op jit(solution)/shard_map/add | solution.py:74
  347.2 2.0 copy.70
  349.2 1.6 copy.80
  350.8 1.7 copy.69
  (255 shorter events, 30.5 us)
Async XLA Ops:
  7.2 135.0 %copy-start = (bf16[4,128,256]{2,1,0:T(8,128)(2,1)S(1)}, bf16[4,128,256]{2,1,0:T(8,128)(2,1)}, u32[]{:S(2)}) copy-start(bf16[4,128,256]{2,1,0:T(8,128)(2,1)} %param.6) | copy-start | bytes 786436
  7.2 130.0 %all-gather.2.cloned.1.call-start = ((), (), s32[]{:S(2)}) async-start(), calls=%async_computation.1 | async-start | bytes 3145728 | tf_op jit(solution)/shard_map/all_gather | solution.py:60
  9.3 59.7 %collective-permute-start.8 = (bf16[128,4,1024]{0,2,1:T(8,128)(2,1)S(1)}, bf16[128,4,1024]{0,2,1:T(8,128)(2,1)S(1)}, u32[]{:S(2)}, u32[]{:S(2)}) collective-permute-start(bf16[128,4,1024]{0,2,1:T(8,128)(2,1)S(1)} %copy.40), channel_id=1, source_target_pairs={{8,0},{10,2},{12,4},{14,6},{16,8},{18,10},{20,12},{22,14},{24,16},... | collective-permute-start | bytes 3145736 | tf_op jit(solution)/shard_map/ppermute | solution.py:15
  10.6 62.7 %collective-permute-start.2 = (bf16[128,4,1024]{0,2,1:T(8,128)(2,1)S(1)}, bf16[128,4,1024]{0,2,1:T(8,128)(2,1)}, u32[]{:S(2)}, u32[]{:S(2)}) collective-permute-start(bf16[128,4,1024]{0,2,1:T(8,128)(2,1)S(1)} %copy.40), channel_id=1, source_target_pairs={{2,0},{4,2},{6,4},{8,6},{10,8},{12,10},{14,12},{16,14},{18,16},{20... | collective-permute-start | bytes 3145736 | tf_op jit(solution)/shard_map/ppermute | solution.py:15
  13.2 63.3 %collective-permute-start = (bf16[128,4,1024]{0,2,1:T(8,128)(2,1)S(1)}, bf16[128,4,1024]{0,2,1:T(8,128)(2,1)}, u32[]{:S(2)}, u32[]{:S(2)}) collective-permute-start(bf16[128,4,1024]{0,2,1:T(8,128)(2,1)S(1)} %copy.40), channel_id=1, source_target_pairs={{0,4},{2,6},{4,8},{6,10},{8,12},{10,14},{12,16},{14,18},{16,20},{1... | collective-permute-start | bytes 3145736 | tf_op jit(solution)/shard_map/ppermute | solution.py:15
  18.3 240.8 %all-reduce.2.cloned.1.call-start = ((), (), s32[]{:S(2)}) async-start(), calls=%async_computation.2 | async-start | bytes 1048576 | tf_op jit(solution)/shard_map/psum | solution.py:84
  18.4 33.3 %collective-permute-start.6 = (bf16[128,2,1024]{0,2,1:T(8,128)(2,1)S(1)}, bf16[128,2,1024]{0,2,1:T(8,128)(2,1)S(1)}, u32[]{:S(2)}, u32[]{:S(2)}) collective-permute-start(bf16[128,2,1024]{0,2,1:T(8,128)(2,1)S(1)} %get-tuple-element.118), channel_id=1, source_target_pairs={{0,10},{2,12},{4,14},{6,16},{8,18},{10,20},{12,22},{14,24},{16,26}... | collective-permute-start | bytes 1572872 | tf_op jit(solution)/shard_map/ppermute | solution.py:15
  23.2 42.0 %collective-permute-start.9 = (bf16[128,2,1024]{0,2,1:T(8,128)(2,1)S(1)}, bf16[128,2,1024]{0,2,1:T(8,128)(2,1)S(1)}, u32[]{:S(2)}, u32[]{:S(2)}) collective-permute-start(bf16[128,2,1024]{0,2,1:T(8,128)(2,1)S(1)} %get-tuple-element.119), channel_id=1, source_target_pairs={{10,0},{12,2},{14,4},{16,6},{18,8},{20,10},{22,12},{24,14},{26,16}... | collective-permute-start | bytes 1572872 | tf_op jit(solution)/shard_map/ppermute | solution.py:15
  24.9 104.0 %copy-start.34 = (bf16[128,4,1006]{0,2,1:T(8,128)(2,1)}, bf16[128,4,1006]{0,2,1:T(8,128)(2,1)S(1)}, u32[]{:S(2)}) copy-start(bf16[128,4,1006]{0,2,1:T(8,128)(2,1)S(1)} %get-tuple-element.116) | copy-start | bytes 3090436
  24.9 104.0 %copy-start.36 = (bf16[128,4,1006]{0,2,1:T(8,128)(2,1)}, bf16[128,4,1006]{0,2,1:T(8,128)(2,1)S(1)}, u32[]{:S(2)}) copy-start(bf16[128,4,1006]{0,2,1:T(8,128)(2,1)S(1)} %get-tuple-element.117) | copy-start | bytes 3090436
  25.4 98.5 %copy-start.25 = (bf16[128,4,1012]{0,2,1:T(8,128)(2,1)}, bf16[128,4,1012]{0,2,1:T(8,128)(2,1)S(1)}, u32[]{:S(2)}) copy-start(bf16[128,4,1012]{0,2,1:T(8,128)(2,1)S(1)} %get-tuple-element.108) | copy-start | bytes 3108868
  25.4 98.5 %copy-start.26 = (bf16[128,4,1012]{0,2,1:T(8,128)(2,1)}, bf16[128,4,1012]{0,2,1:T(8,128)(2,1)S(1)}, u32[]{:S(2)}) copy-start(bf16[128,4,1012]{0,2,1:T(8,128)(2,1)S(1)} %get-tuple-element.109) | copy-start | bytes 3108868
  25.8 107.3 %copy-start.15 = (bf16[128,4,1018]{0,2,1:T(8,128)(2,1)}, bf16[128,4,1018]{0,2,1:T(8,128)(2,1)S(1)}, u32[]{:S(2)}) copy-start(bf16[128,4,1018]{0,2,1:T(8,128)(2,1)S(1)} %get-tuple-element.101) | copy-start | bytes 3127300
  25.8 107.3 %copy-start.16 = (bf16[128,4,1018]{0,2,1:T(8,128)(2,1)}, bf16[128,4,1018]{0,2,1:T(8,128)(2,1)S(1)}, u32[]{:S(2)}) copy-start(bf16[128,4,1018]{0,2,1:T(8,128)(2,1)S(1)} %get-tuple-element.100) | copy-start | bytes 3127300
  26.1 107.0 %copy-start.60 = (bf16[128,4,6]{0,2,1:T(8,128)(2,1)}, bf16[128,4,6]{0,2,1:T(8,128)(2,1)S(1)}, u32[]{:S(2)}) copy-start(bf16[128,4,6]{0,2,1:T(8,128)(2,1)S(1)} %get-tuple-element.99) | copy-start | bytes 18436
  26.1 107.0 %copy-start.62 = (bf16[128,4,6]{0,2,1:T(8,128)(2,1)}, bf16[128,4,6]{0,2,1:T(8,128)(2,1)S(1)}, u32[]{:S(2)}) copy-start(bf16[128,4,6]{0,2,1:T(8,128)(2,1)S(1)} %get-tuple-element.98) | copy-start | bytes 18436
  27.2 101.7 %copy-start.69 = (f32[128]{0:T(128)}, f32[128]{0:T(128)S(1)}, u32[]{:S(2)}) copy-start(f32[128]{0:T(128)S(1)} %get-tuple-element.121) | copy-start | bytes 1540
  27.2 101.7 %copy-start.71 = (f32[128]{0:T(128)}, f32[128]{0:T(128)S(1)}, u32[]{:S(2)}) copy-start(f32[128]{0:T(128)S(1)} %get-tuple-element.122) | copy-start | bytes 1540
  27.2 101.7 %copy-start.73 = (f32[128]{0:T(128)}, f32[128]{0:T(128)S(1)}, u32[]{:S(2)}) copy-start(f32[128]{0:T(128)S(1)} %get-tuple-element.123) | copy-start | bytes 1540
  27.2 101.7 %copy-start.75 = (f32[128]{0:T(128)}, f32[128]{0:T(128)S(1)}, u32[]{:S(2)}) copy-start(f32[128]{0:T(128)S(1)} %get-tuple-element.124) | copy-start | bytes 1540
  27.2 101.7 %copy-start.77 = (f32[128]{0:T(128)}, f32[128]{0:T(128)S(1)}, u32[]{:S(2)}) copy-start(f32[128]{0:T(128)S(1)} %get-tuple-element.125) | copy-start | bytes 1540
  27.3 101.7 %copy-start.79 = (f32[128]{0:T(128)}, f32[128]{0:T(128)S(1)}, u32[]{:S(2)}) copy-start(f32[128]{0:T(128)S(1)} %get-tuple-element.126) | copy-start | bytes 1540
  27.3 101.7 %copy-start.81 = (f32[128]{0:T(128)}, f32[128]{0:T(128)S(1)}, u32[]{:S(2)}) copy-start(f32[128]{0:T(128)S(1)} %get-tuple-element.127) | copy-start | bytes 1540
  27.3 101.7 %copy-start.83 = (f32[128]{0:T(128)}, f32[128]{0:T(128)S(1)}, u32[]{:S(2)}) copy-start(f32[128]{0:T(128)S(1)} %get-tuple-element.128) | copy-start | bytes 1540
  27.3 105.8 %copy-start.67 = (f32[128]{0:T(128)}, f32[128]{0:T(128)S(1)}, u32[]{:S(2)}) copy-start(f32[128]{0:T(128)S(1)} %get-tuple-element.120) | copy-start | bytes 1540
  51.7 34.6 %collective-permute-start.7 = (bf16[128,4,1024]{0,2,1:T(8,128)(2,1)S(1)}, bf16[128,4,1024]{0,2,1:T(8,128)(2,1)S(1)}, u32[]{:S(2)}, u32[]{:S(2)}) collective-permute-start(bf16[128,4,1024]{0,2,1:T(8,128)(2,1)S(1)} %copy.40), channel_id=1, source_target_pairs={{0,8},{2,10},{4,12},{6,14},{8,16},{10,18},{12,20},{14,22},{16,24},... | collective-permute-start | bytes 3145736 | tf_op jit(solution)/shard_map/ppermute | solution.py:15
  65.2 53.8 %collective-permute-start.4 = (bf16[128,4,1024]{0,2,1:T(8,128)(2,1)S(1)}, bf16[128,4,1024]{0,2,1:T(8,128)(2,1)S(1)}, u32[]{:S(2)}, u32[]{:S(2)}) collective-permute-start(bf16[128,4,1024]{0,2,1:T(8,128)(2,1)S(1)} %copy.40), channel_id=1, source_target_pairs={{0,6},{2,8},{4,10},{6,12},{8,14},{10,16},{12,18},{14,20},{16,22},{... | collective-permute-start | bytes 3145736 | tf_op jit(solution)/shard_map/ppermute | solution.py:15
  70.0 49.1 %collective-permute-start.3 = (bf16[128,4,1024]{0,2,1:T(8,128)(2,1)S(1)}, bf16[128,4,1024]{0,2,1:T(8,128)(2,1)S(1)}, u32[]{:S(2)}, u32[]{:S(2)}) collective-permute-start(bf16[128,4,1024]{0,2,1:T(8,128)(2,1)S(1)} %copy.40), channel_id=1, source_target_pairs={{4,0},{6,2},{8,4},{10,6},{12,8},{14,10},{16,12},{18,14},{20,16},{2... | collective-permute-start | bytes 3145736 | tf_op jit(solution)/shard_map/ppermute | solution.py:15
  73.3 50.0 %collective-permute-start.5 = (bf16[128,4,1024]{0,2,1:T(8,128)(2,1)S(1)}, bf16[128,4,1024]{0,2,1:T(8,128)(2,1)S(1)}, u32[]{:S(2)}, u32[]{:S(2)}) collective-permute-start(bf16[128,4,1024]{0,2,1:T(8,128)(2,1)S(1)} %copy.40), channel_id=1, source_target_pairs={{6,0},{8,2},{10,4},{12,6},{14,8},{16,10},{18,12},{20,14},{22,16},{... | collective-permute-start | bytes 3145736 | tf_op jit(solution)/shard_map/ppermute | solution.py:15
  76.5 45.3 %collective-permute-start.1 = (bf16[128,4,1024]{0,2,1:T(8,128)(2,1)S(1)}, bf16[128,4,1024]{0,2,1:T(8,128)(2,1)S(1)}, u32[]{:S(2)}, u32[]{:S(2)}) collective-permute-start(bf16[128,4,1024]{0,2,1:T(8,128)(2,1)S(1)} %copy.40), channel_id=1, source_target_pairs={{0,2},{2,4},{4,6},{6,8},{8,10},{10,12},{12,14},{14,16},{16,18},{18... | collective-permute-start | bytes 3145736 | tf_op jit(solution)/shard_map/ppermute | solution.py:15
  86.4 42.6 %copy-start.8 = (bf16[128,6,1024]{0,2,1:T(8,128)(2,1)}, bf16[128,6,1024]{0,2,1:T(8,128)(2,1)S(1)}, u32[]{:S(2)}) copy-start(bf16[128,6,1024]{0,2,1:T(8,128)(2,1)S(1)} %constant_dynamic-update-slice_fusion.4) | copy-start | bytes 4718596
  119.2 13.9 %copy-start.11 = (bf16[128,8,1024]{0,2,1:T(8,128)(2,1)}, bf16[128,8,1024]{0,2,1:T(8,128)(2,1)S(1)}, u32[]{:S(2)}) copy-start(bf16[128,8,1024]{0,2,1:T(8,128)(2,1)S(1)} %constant_dynamic-update-slice_fusion.2) | copy-start | bytes 6291460
  119.2 13.9 %copy-start.64 = (bf16[128,4,6]{0,2,1:T(8,128)(2,1)}, bf16[128,4,6]{0,2,1:T(8,128)(2,1)S(1)}, u32[]{:S(2)}) copy-start(bf16[128,4,6]{0,2,1:T(8,128)(2,1)S(1)} %get-tuple-element.46) | copy-start | bytes 18436
  122.0 11.2 %copy-start.10 = (bf16[128,8,1024]{0,2,1:T(8,128)(2,1)}, bf16[128,8,1024]{0,2,1:T(8,128)(2,1)S(1)}, u32[]{:S(2)}) copy-start(bf16[128,8,1024]{0,2,1:T(8,128)(2,1)S(1)} %constant_dynamic-update-slice_fusion) | copy-start | bytes 6291460
  141.9 207.3 %reduce-scatter.4.cloned.1.call-start = ((), (), s32[]{:S(2)}) async-start(), calls=%async_computation.3 | async-start | bytes 3145728
  154.1 32.1 %copy-start.2 = (bf16[4,128,4,1024]{1,3,2,0:T(8,128)(2,1)}, bf16[4,128,4,1024]{1,3,2,0:T(8,128)(2,1)S(1)}, u32[]{:S(2)}) copy-start(bf16[4,128,4,1024]{1,3,2,0:T(8,128)(2,1)S(1)} %convolution_convert_fusion) | copy-start | bytes 12582916
  159.8 19.9 %copy-start.13 = (bf16[128,4,1024]{0,2,1:T(8,128)(2,1)}, bf16[128,4,1024]{0,2,1:T(8,128)(2,1)S(1)}, u32[]{:S(2)}) copy-start(bf16[128,4,1024]{0,2,1:T(8,128)(2,1)S(1)} %get-tuple-element.41) | copy-start | bytes 3145732
  162.0 124.9 %collective-permute-start.13 = (bf16[128,4,1024]{0,2,1:T(8,128)(2,1)S(1)}, bf16[128,4,1024]{0,2,1:T(8,128)(2,1)}, u32[]{:S(2)}, u32[]{:S(2)}) collective-permute-start(bf16[128,4,1024]{0,2,1:T(8,128)(2,1)S(1)} %get-tuple-element.39), channel_id=1, source_target_pairs={{0,2},{2,4},{4,6},{6,8},{8,10},{10,12},{12,14},{14,16},{16,18},{18... | collective-permute-start | bytes 3145736 | tf_op jit(solution)/shard_map/ppermute | solution.py:15
  174.8 102.1 %collective-permute-start.10 = (bf16[128,4,1024]{0,2,1:T(8,128)(2,1)S(1)}, bf16[128,4,1024]{0,2,1:T(8,128)(2,1)}, u32[]{:S(2)}, u32[]{:S(2)}) collective-permute-start(bf16[128,4,1024]{0,2,1:T(8,128)(2,1)S(1)} %get-tuple-element.39), channel_id=1, source_target_pairs={{2,0},{4,2},{6,4},{8,6},{10,8},{12,10},{14,12},{16,14},{18,16},{20... | collective-permute-start | bytes 3145736 | tf_op jit(solution)/shard_map/ppermute | solution.py:15
  176.7 103.6 %collective-permute-start.16 = (bf16[128,4,1024]{0,2,1:T(8,128)(2,1)S(1)}, bf16[128,4,1024]{0,2,1:T(8,128)(2,1)}, u32[]{:S(2)}, u32[]{:S(2)}) collective-permute-start(bf16[128,4,1024]{0,2,1:T(8,128)(2,1)S(1)} %get-tuple-element.40), channel_id=1, source_target_pairs={{8,0},{10,2},{12,4},{14,6},{16,8},{18,10},{20,12},{22,14},{24,16},... | collective-permute-start | bytes 3145736 | tf_op jit(solution)/shard_map/ppermute | solution.py:15
  183.2 77.8 %collective-permute-start.12 = (bf16[128,2,1024]{0,2,1:T(8,128)(2,1)}, bf16[128,2,1024]{0,2,1:T(8,128)(2,1)}, u32[]{:S(2)}, u32[]{:S(2)}) collective-permute-start(bf16[128,2,1024]{0,2,1:T(8,128)(2,1)} %get-tuple-element.95), channel_id=1, source_target_pairs={{0,4},{2,6},{4,8},{6,10},{8,12},{10,14},{12,16},{14,18},{16,20},{1... | collective-permute-start | bytes 1572872 | tf_op jit(solution)/shard_map/ppermute | solution.py:15
  194.8 82.1 %copy-start.14 = (bf16[128,4,1024]{0,2,1:T(8,128)(2,1)S(1)}, bf16[128,4,1024]{0,2,1:T(8,128)(2,1)}, u32[]{:S(2)}) copy-start(bf16[128,4,1024]{0,2,1:T(8,128)(2,1)} %copy-done.13) | copy-start | bytes 3145732
  253.3 15.5 %collective-permute-start.18 = (bf16[128,2,1024]{0,2,1:T(8,128)(2,1)}, bf16[128,2,1024]{0,2,1:T(8,128)(2,1)}, u32[]{:S(2)}, u32[]{:S(2)}) collective-permute-start(bf16[128,2,1024]{0,2,1:T(8,128)(2,1)} %get-tuple-element.97), channel_id=1, source_target_pairs={{0,10},{2,12},{4,14},{6,16},{8,18},{10,20},{12,22},{14,24},{16,26}... | collective-permute-start | bytes 1572872 | tf_op jit(solution)/shard_map/ppermute | solution.py:15
  261.0 24.3 %collective-permute-start.11 = (bf16[128,2,1024]{0,2,1:T(8,128)(2,1)}, bf16[128,2,1024]{0,2,1:T(8,128)(2,1)S(1)}, u32[]{:S(2)}, u32[]{:S(2)}) collective-permute-start(bf16[128,2,1024]{0,2,1:T(8,128)(2,1)} %get-tuple-element.94), channel_id=1, source_target_pairs={{4,0},{6,2},{8,4},{10,6},{12,8},{14,10},{16,12},{18,14},{20,16},{2... | collective-permute-start | bytes 1572872 | tf_op jit(solution)/shard_map/ppermute | solution.py:15
  268.8 29.8 %collective-permute-start.19 = (bf16[128,4,1024]{0,2,1:T(8,128)(2,1)S(1)}, bf16[128,4,1024]{0,2,1:T(8,128)(2,1)S(1)}, u32[]{:S(2)}, u32[]{:S(2)}) collective-permute-start(bf16[128,4,1024]{0,2,1:T(8,128)(2,1)S(1)} %get-tuple-element.40), channel_id=1, source_target_pairs={{0,8},{2,10},{4,12},{6,14},{8,16},{10,18},{12,20},{14,22},{16,24},... | collective-permute-start | bytes 3145736 | tf_op jit(solution)/shard_map/ppermute | solution.py:15
  276.9 42.8 %collective-permute-start.15 = (bf16[128,4,1024]{0,2,1:T(8,128)(2,1)S(1)}, bf16[128,4,1024]{0,2,1:T(8,128)(2,1)S(1)}, u32[]{:S(2)}, u32[]{:S(2)}) collective-permute-start(bf16[128,4,1024]{0,2,1:T(8,128)(2,1)S(1)} %copy-done.14), channel_id=1, source_target_pairs={{0,6},{2,8},{4,10},{6,12},{8,14},{10,16},{12,18},{14,20},{16,22},{... | collective-permute-start | bytes 3145736 | tf_op jit(solution)/shard_map/ppermute | solution.py:15
  280.3 39.4 %collective-permute-start.14 = (bf16[128,4,1024]{0,2,1:T(8,128)(2,1)S(1)}, bf16[128,4,1024]{0,2,1:T(8,128)(2,1)S(1)}, u32[]{:S(2)}, u32[]{:S(2)}) collective-permute-start(bf16[128,4,1024]{0,2,1:T(8,128)(2,1)S(1)} %copy-done.14), channel_id=1, source_target_pairs={{6,0},{8,2},{10,4},{12,6},{14,8},{16,10},{18,12},{20,14},{22,16},{... | collective-permute-start | bytes 3145736 | tf_op jit(solution)/shard_map/ppermute | solution.py:15
  285.3 40.9 %collective-permute-start.17 = (bf16[128,2,1024]{0,2,1:T(8,128)(2,1)S(1)}, bf16[128,2,1024]{0,2,1:T(8,128)(2,1)S(1)}, u32[]{:S(2)}, u32[]{:S(2)}) collective-permute-start(bf16[128,2,1024]{0,2,1:T(8,128)(2,1)S(1)} %copy-done.53), channel_id=1, source_target_pairs={{10,0},{12,2},{14,4},{16,6},{18,8},{20,10},{22,12},{24,14},{26,16}... | collective-permute-start | bytes 1572872 | tf_op jit(solution)/shard_map/ppermute | solution.py:15
  (60 other events, 287.2 us)
Sparse Core Ops, SparseCore 0:
  18.4 34.1 all-gather.1
  142.0 102.9 all-reduce.1
  247.3 32.5 reduce-scatter.3
where the time goes:
time: 360 us; the launch traced here: 359 us
  waiting for transfers between devices  104 us (29%)
  starting transfers between devices  81.4 us (23%)
  blocking collectives  57.9 us (16%)
  local copies, waits for them, and re-layouts  45.4 us (13%)
  other arithmetic  43.3 us (12%)
  between operations  15.4 us (4%)
  matrix products  12.1 us (3%)
    ppermute x20, waiting for transfers between devices, shifted(): return lax.ppermute(block, axis, route)  103 us
    ppermute x20, starting transfers between devices, shifted(): return lax.ppermute(block, axis, route)  81.1 us
    psum x1, blocking collectives, local(): depth_total, point_total = lax.psum((depth_local, point_local), 'band')  57.9 us
    unnamed x185, local copies, waits for them, and re-layouts  27.5 us
    add x1, other arithmetic, local(): grad_input + kernel[which, tap_index][:, None, None] * window(grad_wide,...  15.4 us
    reduce_sum x4, other arithmetic, local(): jnp.sum(grad_f * window(feat_wide, 18, spacing, row_step, col_step, heigh...  13.9 us
    another operation x3, other arithmetic, local(): stacked = jnp.stack(branches)  12.1 us
    slice x36, local copies, waits for them, and re-layouts, window(): return jnp.roll(piece, -col_step * spacing, axis=-1)  11.5 us
  transfers between devices with their start and end apart: 23, of which 8 were waited for; matrix products, arithmetic and copies ran while one was open for 24% of the time, Pallas kernels for 0%

commit v1 on v0

v1 whole, which is shorter than its diff:
```python
import jax
import jax.numpy as jnp
from jax import lax
from jax.sharding import PartitionSpec as P

GSCALE = 1024


dilations = (6, 12, 18)


def shifted(block, axis, distance):
    devices = range(lax.axis_size(axis))
    route = [(i - distance, i) for i in devices if i - distance in devices]
    if not route:
        return jnp.zeros_like(block)
    return lax.ppermute(block, axis, route)


def from_device(block, ahead):
    return block if ahead == 0 else shifted(block, "band", -ahead)


def rows_at(field, offset):
    height = field.shape[1]
    ahead, start = divmod(offset, height)
    if start == 0:
        return from_device(field, ahead)
    return jnp.concatenate(
        [from_device(field[:, start:], ahead), from_device(field[:, :start], ahead + 1)], axis=1
    )


def local(features, depth_kernel, pointwise, cotangent):
    kernel = depth_kernel.astype(jnp.float32)
    feat_rows = {0: features}
    for spacing in dilations:
        for side in (-1, 1):
            feat_rows[side * spacing] = rows_at(features, side * spacing)
    feat_rows = {k: v.astype(jnp.float32) for k, v in feat_rows.items()}
    branches = [features]
    for which, spacing in enumerate(dilations):
        total = jnp.zeros(features.shape, jnp.float32)
        for tap_index in range(9):
            row_step = tap_index // 3 - 1
            col_step = tap_index % 3 - 1
            total = total + kernel[which, tap_index][:, None, None] * jnp.roll(
                feat_rows[row_step * spacing], -col_step * spacing, axis=-1
            )
        branches.append(total.astype(jnp.bfloat16))
    stacked = jnp.stack(branches)
    output = lax.psum_scatter(
        jnp.einsum("bchw,bco->ohw", stacked, pointwise, preferred_element_type=jnp.float32).astype(
            jnp.bfloat16
        ),
        "chan",
        scatter_dimension=0,
        tiled=True,
    )
    cot_full = lax.all_gather(cotangent, "chan", axis=0, tiled=True)
    grad_sum = jnp.einsum("bco,ohw->bchw", pointwise, cot_full, preferred_element_type=jnp.float32)
    point_local = jnp.einsum("bchw,ohw->bco", stacked, cot_full, preferred_element_type=jnp.float32)
    grad_branches = grad_sum.astype(jnp.bfloat16)
    grad_input = grad_branches[0].astype(jnp.float32)
    depth_rows = []
    for which, spacing in enumerate(dilations):
        grad_field = grad_branches[which + 1]
        grad_f = grad_field.astype(jnp.float32)
        grad_rows = {0: grad_f}
        for side in (-1, 1):
            grad_rows[side * spacing] = rows_at(grad_field, side * spacing).astype(jnp.float32)
        tap_rows = []
        for tap_index in range(9):
            row_step = tap_index // 3 - 1
            col_step = tap_index % 3 - 1
            grad_input = grad_input + kernel[which, tap_index][:, None, None] * jnp.roll(
                grad_rows[-row_step * spacing], col_step * spacing, axis=-1
            )
            tap_rows.append(
                jnp.sum(
                    grad_f * jnp.roll(feat_rows[row_step * spacing], -col_step * spacing, axis=-1),
                    axis=(1, 2),
                )
            )
        depth_rows.append(jnp.stack(tap_rows))
    depth_local = jnp.stack(depth_rows)
    flat = jnp.concatenate([depth_local.reshape(-1), point_local.reshape(-1)])
    flat = lax.psum(flat, "band")
    depth_total = flat[: depth_local.size].reshape(depth_local.shape)
    point_total = flat[depth_local.size :].reshape(point_local.shape)
    return (output, grad_input, depth_total / GSCALE, point_total / GSCALE)


def solution(mesh):
    return jax.shard_map(
        local,
        mesh=mesh,
        in_specs=(
            P("chan", "band", None),
            P(None, None, "chan"),
            P(None, "chan", None),
            P("chan", "band", None),
        ),
        out_specs=(
            P("chan", "band", None),
            P("chan", "band", None),
            P(None, None, "chan"),
            P(None, "chan", None),
        ),
        check_vma=False,
    )
```

time: 360 us -> 349 us (0.969)
  blocking collectives: 57.9 us -> 0 us
  other arithmetic: 43.3 us -> 67.8 us
  local copies, waits for them, and re-layouts: 45.4 us -> 57.9 us
  waiting for transfers between devices: 104 us -> 116 us
  matrix products: 12.1 us -> 7.48 us
    psum x1, waiting for transfers between devices: 0.01 us -> 62.5 us  [local(): flat = lax.psum(flat, 'band')]
    psum x1 -> x0, blocking collectives: 57.9 us -> none  [local(): depth_total, point_total = lax.psum((depth_local, point_local), 'band')]
    ppermute x20, waiting for transfers between devices: 103 us -> 53.6 us  [shifted(): return lax.ppermute(block, axis, route)]
    slice x39, local copies, waits for them, and re-layouts: 13.8 us -> 28.8 us  [the longest x18 17.4 us: local(): jnp.roll(grad_rows[-row_step * spacing], col_step * spacing, axis=-1)]
    convert_element_type x0 -> x9, other arithmetic: none -> 8.92 us  [the longest x1 3.9 us: local(): grad_f = grad_field.astype(jnp.float32)]
    reduce_sum x4, other arithmetic: 13.9 us -> 21.7 us  [local(): jnp.sum(grad_f * jnp.roll(feat_rows[row_step * spacing], -col_step * spac...]
    unnamed x185 -> x220, local copies, waits for them, and re-layouts: 27.5 us -> 20.7 us
    another operation x3, local copies, waits for them, and re-layouts: 0.12 us -> 5.21 us  [local(): depth_rows.append(jnp.stack(tap_rows))]
  transfers between devices with their start and end apart: 23 -> 23, of which waited for: 8 -> 5; matrix products, arithmetic and copies ran while one was open for 24% -> 24% of each run, Pallas kernels for 0% -> 0%
where the time goes in v1:
time: 349 us; the launch traced here: 347 us
  waiting for transfers between devices  116 us (33%)
  starting transfers between devices  82.4 us (24%)
  other arithmetic  67.8 us (19%)
  local copies, waits for them, and re-layouts  57.9 us (17%)
  between operations  15.5 us (4%)
  matrix products  7.48 us (2%)
    ppermute x20, starting transfers between devices, shifted(): return lax.ppermute(block, axis, route)  82.3 us
    psum x1, waiting for transfers between devices, local(): flat = lax.psum(flat, 'band')  62.5 us
    ppermute x20, waiting for transfers between devices, shifted(): return lax.ppermute(block, axis, route)  53.6 us
    reduce_sum x4, other arithmetic, local(): jnp.sum(grad_f * jnp.roll(feat_rows[row_step * spacing], -col_step * spac...  21.7 us
    unnamed x220, local copies, waits for them, and re-layouts  20.7 us
    slice x18, local copies, waits for them, and re-layouts, local(): jnp.roll(grad_rows[-row_step * spacing], col_step * spacing, axis=-1)  17.4 us
    another operation x3, other arithmetic, local(): stacked = jnp.stack(branches)  17.2 us
    add x1, other arithmetic, local(): grad_input + kernel[which, tap_index][:, None, None] * jnp.roll(grad_rows...  15.6 us
  transfers between devices with their start and end apart: 23, of which 5 were waited for; matrix products, arithmetic and copies ran while one was open for 24% of the time, Pallas kernels for 0%

profile of v1, /device:TPU:3, one launch (start us, length us, event | category | flops | bytes accessed | tf_op | source)
XLA Modules:
  0.0 347.3 jit_solution(9047192822826043685)
XLA Ops:
  7.2 2.0 copy.35
  11.5 5.8 %collective-permute-start.6 = (bf16[128,2,1024]{0,2,1:T(8,128)(2,1)}, bf16[128,2,1024]{0,2,1:T(8,128)(2,1)S(1)}, u32[]{:S(2)}, u32[]{:S(2)}) collective-permute-start(bf16[128,2,1024]{0,2,1:T(8,128)(2,1)} %get-tuple-element.125), channel_id=1, source_target_pairs={{0,10},{2,12},{4,14},{6,16},{8,18},{10,20},{12,22},{14,24},{16,26}... | collective-permute-start | bytes 1572872 | tf_op jit(solution)/shard_map/ppermute | solution.py:17
  17.4 1.9 collective-permute-start.2
  19.3 3.1 collective-permute-start
  23.8 3.3 collective-permute-start.7
  32.2 20.4 %collective-permute-done.7 = bf16[128,2,1024]{0,2,1:T(8,128)(2,1)S(1)} collective-permute-done((bf16[128,2,1024]{0,2,1:T(8,128)(2,1)}, bf16[128,2,1024]{0,2,1:T(8,128)(2,1)S(1)}, u32[]{:S(2)}, u32[]{:S(2)}) %collective-permute-start.7) | collective-permute-done | bytes 524320 | tf_op jit(solution)/shard_map/ppermute | solution.py:17
  52.7 1.9 collective-permute-start.3
  54.8 2.3 fusion.104
  57.1 3.6 %collective-permute-start.1 = (bf16[128,2,1024]{0,2,1:T(8,128)(2,1)}, bf16[128,2,1024]{0,2,1:T(8,128)(2,1)S(1)}, u32[]{:S(2)}, u32[]{:S(2)}) collective-permute-start(bf16[128,2,1024]{0,2,1:T(8,128)(2,1)} %get-tuple-element.126), channel_id=1, source_target_pairs={{0,2},{2,4},{4,6},{6,8},{8,10},{10,12},{12,14},{14,16},{16,18},{18... | collective-permute-start | bytes 1572872 | tf_op jit(solution)/shard_map/ppermute | solution.py:17
  60.7 1.9 collective-permute-start.5
  62.8 2.2 fusion.106
  65.0 10.3 %collective-permute-start.4 = (bf16[128,4,1024]{0,2,1:T(8,128)(2,1)S(1)}, bf16[128,4,1024]{0,2,1:T(8,128)(2,1)S(1)}, u32[]{:S(2)}, u32[]{:S(2)}) collective-permute-start(bf16[128,4,1024]{0,2,1:T(8,128)(2,1)S(1)} %copy.35), channel_id=1, source_target_pairs={{0,6},{2,8},{4,10},{6,12},{8,14},{10,16},{12,18},{14,20},{16,22},{... | collective-permute-start | bytes 3145736 | tf_op jit(solution)/shard_map/ppermute | solution.py:17
  80.7 7.1 %fusion.75 = bf16[1,128,4,1024]{1,3,0,2:T(8,128)(2,1)} fusion(f32[128,4,18]{0,2,1:T(8,128)S(1)} %get-tuple-element.90, f32[128,4,1006]{0,2,1:T(8,128)} %get-tuple-element.92, f32[128]{0:T(128)S(1)} %get-tuple-element.128, f32[128]{0:T(128)S(1)} %get-tuple-element.129, f32[128,4,1006]{0,2,1:T(8,128)} %get-tuple-element.91, ...), kind=kLoop, calls=%fused_computation.159 | loop fusion | flops 15204352 | bytes 16781824 | tf_op jit(solution)/shard_map/stack | solution.py:51
  87.9 5.8 %fusion.77 = bf16[1,128,4,1024]{1,3,0,2:T(8,128)(2,1)} fusion(f32[128,4,6]{0,2,1:T(8,128)S(1)} %get-tuple-element.82, f32[128,4,1018]{0,2,1:T(8,128)S(1)} %get-tuple-element.84, f32[128]{0:T(128)} %get-tuple-element.147, f32[128]{0:T(128)} %get-tuple-element.148, f32[128,4,1018]{0,2,1:T(8,128)S(1)} %get-tuple-element.83, ...), kind=kLoop, calls=%fused_computation.161 | loop fusion | flops 15204352 | bytes 16781824 | tf_op jit(solution)/shard_map/stack | solution.py:51
  93.8 4.0 %collective-permute-done.4 = bf16[128,4,1024]{0,2,1:T(8,128)(2,1)S(1)} collective-permute-done((bf16[128,4,1024]{0,2,1:T(8,128)(2,1)S(1)}, bf16[128,4,1024]{0,2,1:T(8,128)(2,1)S(1)}, u32[]{:S(2)}, u32[]{:S(2)}) %collective-permute-start.4) | collective-permute-done | bytes 1048608 | tf_op jit(solution)/shard_map/ppermute | solution.py:17
  98.2 2.1 fusion.120
  101.7 4.3 %fusion.76 = bf16[1,128,4,1024]{1,3,0,2:T(8,128)(2,1)} fusion(f32[128,4,12]{0,2,1:T(8,128)S(1)} %get-tuple-element.118, f32[128,4,1012]{0,2,1:T(8,128)S(1)} %get-tuple-element.120, f32[128]{0:T(128)S(1)} %copy-done.97, bf16[128,4,1024]{0,2,1:T(8,128)(2,1)S(1)} %collective-permute-done.5, f32[128]{0:T(128)S(1)} %copy-done.98, ...), kind=kLoop, calls=%fused_computation.160 | loop fusion | flops 14155776 | bytes 16781824 | tf_op jit(solution)/shard_map/stack | solution.py:51
  106.0 3.0 convolution_convert_fusion
  109.5 5.9 %fusion.47 = (f32[128]{0:T(128)}, f32[128]{0:T(128)}, f32[128]{0:T(128)}, f32[128]{0:T(128)}, f32[128]{0:T(128)}, /*index=5*/f32[128]{0:T(128)}) fusion(f32[128,4,1018]{0,2,1:T(8,128)S(1)} %copy-done.15, f32[128,4,6]{0,2,1:T(8,128)S(1)} %copy-done.84, bf16[4,128,4,1024]{1,3,2,0:T(8,128)(2,1)S(1)} %convolution_convert_fusion, ...), kind=kLoop, calls=%fused_computation.83 | loop fusion | flops 10484992 | bytes 14683136 | tf_op jit(solution)/shard_map/reduce_sum | solution.py:80
  118.9 4.5 %fusion.48 = (f32[128]{0:T(128)}, f32[128]{0:T(128)}, f32[128]{0:T(128)}, f32[128]{0:T(128)}, f32[128]{0:T(128)}, /*index=5*/f32[128]{0:T(128)}, f32[128]{0:T(128)}) fusion(bf16[128,2,1024]{0,2,1:T(8,128)(2,1)S(1)} %copy-done.41, bf16[128,2,1024]{0,2,1:T(8,128)(2,1)} %collective-permute-done.2, bf16[4,128,4,1024]{1,3,2,0:T(8,128)(2,1)S(1)} %convolution_convert_fusion, ...), kind=kLoop, calls=%fused_computation.84 | loop fusion | flops 13630592 | bytes 13635072 | tf_op jit(solution)/shard_map/reduce_sum | solution.py:80
  123.5 4.9 %fusion.45 = (f32[128]{0:T(128)}, f32[128]{0:T(128)}, f32[128]{0:T(128)}, f32[128]{0:T(128)}, f32[128]{0:T(128)}, /*index=5*/f32[128]{0:T(128)}, f32[128]{0:T(128)}, f32[128]{0:T(128)}) fusion(bf16[128,4,1024]{0,2,1:T(8,128)(2,1)S(1)} %copy.35, bf16[4,128,4,1024]{1,3,2,0:T(8,128)(2,1)S(1)} %convolution_convert_fusion, f32[128,4,6]{0,2,1:T(8,128)S(1)} %copy-done.77, ...), kind=kLoop, calls=%fused_computation.81 | loop fusion | flops 13630464 | bytes 13635584 | tf_op jit(solution)/shard_map/reduce_sum | solution.py:80
  128.4 2.5 stack.142
  130.9 6.4 %fusion.49 = (f32[128]{0:T(128)}, f32[128]{0:T(128)}, f32[128]{0:T(128)}, f32[128]{0:T(128)}, f32[128]{0:T(128)}, /*index=5*/f32[128]{0:T(128)}) fusion(f32[128,4,6]{0,2,1:T(8,128)} %copy-done.78, f32[128,4,1018]{0,2,1:T(8,128)S(1)} %copy-done.13, bf16[4,128,4,1024]{1,3,2,0:T(8,128)(2,1)} %copy-done.2, f32[128,4,18]{0,2,1:T(8,128)} %copy-done.57, ...), kind=kLoop, calls=%fused_computation.85 | loop fusion | flops 11009280 | bytes 13634560 | tf_op jit(solution)/shard_map/reduce_sum | solution.py:80
  140.7 1.9 pad_maximum_fusion.21
  142.7 3.1 bitcast_convert_fusion
  145.8 3.0 copy.56
  148.8 3.9 %fusion.84 = (f32[128,4,1024]{0,2,1:T(8,128)S(1)}, f32[128,4,1024]{0,2,1:T(8,128)S(1)}, f32[128,4,1024]{0,2,1:T(8,128)S(1)}, bf16[128,4,1024]{0,2,1:T(8,128)(2,1...) fusion(bf16[4,128,4,1024]{1,3,2,0:T(8,128)(2,1)} %copy-done.2), kind=kLoop, calls=%fused_computation.199 | loop fusion | flops 1572864 | bytes 12582912 | tf_op jit(solution)/shard_map/convert_element_type | solution.py:68
  153.8 12.2 %collective-permute-start.18 = (bf16[128,2,1024]{0,2,1:T(8,128)(2,1)}, bf16[128,2,1024]{0,2,1:T(8,128)(2,1)S(1)}, u32[]{:S(2)}, u32[]{:S(2)}) collective-permute-start(bf16[128,2,1024]{0,2,1:T(8,128)(2,1)} %get-tuple-element.93), channel_id=1, source_target_pairs={{0,10},{2,12},{4,14},{6,16},{8,18},{10,20},{12,22},{14,24},{16,26}... | collective-permute-start | bytes 1572872 | tf_op jit(solution)/shard_map/ppermute | solution.py:17
  167.3 4.0 %collective-permute-start.19 = (bf16[128,2,1024]{0,2,1:T(8,128)(2,1)}, bf16[128,2,1024]{0,2,1:T(8,128)(2,1)S(1)}, u32[]{:S(2)}, u32[]{:S(2)}) collective-permute-start(bf16[128,2,1024]{0,2,1:T(8,128)(2,1)} %get-tuple-element.94), channel_id=1, source_target_pairs={{0,8},{2,10},{4,12},{6,14},{8,16},{10,18},{12,20},{14,22},{16,24},... | collective-permute-start | bytes 1572872 | tf_op jit(solution)/shard_map/ppermute | solution.py:17
  172.6 2.3 fusion.88
  174.9 2.4 fusion.92
  177.3 2.4 fusion.96
  180.7 14.3 %collective-permute-start.12 = (bf16[128,2,1024]{0,2,1:T(8,128)(2,1)}, bf16[128,2,1024]{0,2,1:T(8,128)(2,1)}, u32[]{:S(2)}, u32[]{:S(2)}) collective-permute-start(bf16[128,2,1024]{0,2,1:T(8,128)(2,1)} %get-tuple-element.103), channel_id=1, source_target_pairs={{0,4},{2,6},{4,8},{6,10},{8,12},{10,14},{12,16},{14,18},{16,20},{1... | collective-permute-start | bytes 1572872 | tf_op jit(solution)/shard_map/ppermute | solution.py:17
  195.0 62.5 %all-reduce.2.cloned.1.call-done = f32[134528]{0:T(1024)} async-done(((f32[134528]{0:T(1024)}), f32[134528]{0:T(1024)}) %all-reduce.2.cloned.1.call-update) | async-done | bytes 538128 | tf_op jit(solution)/shard_map/psum | solution.py:88
  260.9 2.8 collective-permute-start.10
  263.7 4.5 %collective-permute-start.13 = (bf16[128,2,1024]{0,2,1:T(8,128)(2,1)}, bf16[128,2,1024]{0,2,1:T(8,128)(2,1)S(1)}, u32[]{:S(2)}, u32[]{:S(2)}) collective-permute-start(bf16[128,2,1024]{0,2,1:T(8,128)(2,1)} %get-tuple-element.104), channel_id=1, source_target_pairs={{0,2},{2,4},{4,6},{6,8},{8,10},{10,12},{12,14},{14,16},{16,18},{18... | collective-permute-start | bytes 1572872 | tf_op jit(solution)/shard_map/ppermute | solution.py:17
  268.4 2.3 fusion.90
  270.7 1.9 collective-permute-start.11
  272.7 3.0 collective-permute-start.15
  275.8 2.2 fusion.86
  278.0 2.7 collective-permute-start.14
  280.7 6.8 %collective-permute-done.11 = bf16[128,2,1024]{0,2,1:T(8,128)(2,1)S(1)} collective-permute-done((bf16[128,2,1024]{0,2,1:T(8,128)(2,1)}, bf16[128,2,1024]{0,2,1:T(8,128)(2,1)S(1)}, u32[]{:S(2)}, u32[]{:S(2)}) %collective-permute-start.11) | collective-permute-done | bytes 524320 | tf_op jit(solution)/shard_map/ppermute | solution.py:17
  290.2 22.4 %collective-permute-done.15 = bf16[128,4,1024]{0,2,1:T(8,128)(2,1)S(1)} collective-permute-done((bf16[128,4,1024]{0,2,1:T(8,128)(2,1)S(1)}, bf16[128,4,1024]{0,2,1:T(8,128)(2,1)S(1)}, u32[]{:S(2)}, u32[]{:S(2)}) %collective-permute-start.15) | collective-permute-done | bytes 1048608 | tf_op jit(solution)/shard_map/ppermute | solution.py:17
  312.7 2.2 fusion.111
  314.9 2.4 fusion.109
  319.9 15.6 %fusion.40 = f32[128,4,1024]{0,2,1:T(8,128)S(1)} fusion(f32[128,4,6]{0,2,1:T(8,128)S(1)} %get-tuple-element.74, f32[128,4,1018]{0,2,1:T(8,128)S(1)} %get-tuple-element.76, f32[128,4,1018]{0,2,1:T(8,128)S(1)} %get-tuple-element.75, f32[128,4,6]{0,2,1:T(8,128)S(1)} %get-tuple-element.73, f32[128,4,6]{0,2,1:T(8,128)S(1)} %get-tuple-element.70, ...), kind=kLoop, calls=%fused_computation.76 | loop fusion | flops 45088768 | bytes 50345472 | tf_op jit(solution)/shard_map/add | solution.py:76
  335.5 2.0 copy.47
  339.0 1.7 copy.46
  (293 shorter events, 38.4 us)
Async XLA Ops:
  7.2 98.8 %copy-start = (bf16[4,128,256]{2,1,0:T(8,128)(2,1)S(1)}, bf16[4,128,256]{2,1,0:T(8,128)(2,1)}, u32[]{:S(2)}) copy-start(bf16[4,128,256]{2,1,0:T(8,128)(2,1)} %param.6) | copy-start | bytes 786436
  7.2 98.7 %all-gather.2.cloned.1.call-start = ((), (), s32[]{:S(2)}) async-start(), calls=%async_computation.1 | async-start | bytes 3145728 | tf_op jit(solution)/shard_map/all_gather | solution.py:60
  10.2 46.8 %collective-permute-start.8 = (bf16[128,2,1024]{0,2,1:T(8,128)(2,1)}, bf16[128,2,1024]{0,2,1:T(8,128)(2,1)S(1)}, u32[]{:S(2)}, u32[]{:S(2)}) collective-permute-start(bf16[128,2,1024]{0,2,1:T(8,128)(2,1)} %get-tuple-element.125), channel_id=1, source_target_pairs={{8,0},{10,2},{12,4},{14,6},{16,8},{18,10},{20,12},{22,14},{24,16},... | collective-permute-start | bytes 1572872 | tf_op jit(solution)/shard_map/ppermute | solution.py:17
  11.5 19.4 %collective-permute-start.6 = (bf16[128,2,1024]{0,2,1:T(8,128)(2,1)}, bf16[128,2,1024]{0,2,1:T(8,128)(2,1)S(1)}, u32[]{:S(2)}, u32[]{:S(2)}) collective-permute-start(bf16[128,2,1024]{0,2,1:T(8,128)(2,1)} %get-tuple-element.125), channel_id=1, source_target_pairs={{0,10},{2,12},{4,14},{6,16},{8,18},{10,20},{12,22},{14,24},{16,26}... | collective-permute-start | bytes 1572872 | tf_op jit(solution)/shard_map/ppermute | solution.py:17
  17.4 47.6 %collective-permute-start.2 = (bf16[128,2,1024]{0,2,1:T(8,128)(2,1)}, bf16[128,2,1024]{0,2,1:T(8,128)(2,1)}, u32[]{:S(2)}, u32[]{:S(2)}) collective-permute-start(bf16[128,2,1024]{0,2,1:T(8,128)(2,1)} %get-tuple-element.125), channel_id=1, source_target_pairs={{2,0},{4,2},{6,4},{8,6},{10,8},{12,10},{14,12},{16,14},{18,16},{20... | collective-permute-start | bytes 1572872 | tf_op jit(solution)/shard_map/ppermute | solution.py:17
  19.3 57.7 %collective-permute-start = (bf16[128,2,1024]{0,2,1:T(8,128)(2,1)}, bf16[128,2,1024]{0,2,1:T(8,128)(2,1)}, u32[]{:S(2)}, u32[]{:S(2)}) collective-permute-start(bf16[128,2,1024]{0,2,1:T(8,128)(2,1)} %get-tuple-element.125), channel_id=1, source_target_pairs={{0,4},{2,6},{4,8},{6,10},{8,12},{10,14},{12,16},{14,18},{16,20},{1... | collective-permute-start | bytes 1572872 | tf_op jit(solution)/shard_map/ppermute | solution.py:17
  23.8 233.7 %all-reduce.2.cloned.1.call-start = ((), (), s32[]{:S(2)}) async-start(), calls=%async_computation.2 | async-start | bytes 1081344 | tf_op jit(solution)/shard_map/psum | solution.py:88
  23.8 28.8 %collective-permute-start.7 = (bf16[128,2,1024]{0,2,1:T(8,128)(2,1)}, bf16[128,2,1024]{0,2,1:T(8,128)(2,1)S(1)}, u32[]{:S(2)}, u32[]{:S(2)}) collective-permute-start(bf16[128,2,1024]{0,2,1:T(8,128)(2,1)} %get-tuple-element.126), channel_id=1, source_target_pairs={{0,8},{2,10},{4,12},{6,14},{8,16},{10,18},{12,20},{14,22},{16,24},... | collective-permute-start | bytes 1572872 | tf_op jit(solution)/shard_map/ppermute | solution.py:17
  27.1 60.8 %copy-start.74 = (f32[128,4,6]{0,2,1:T(8,128)}, f32[128,4,6]{0,2,1:T(8,128)S(1)}, u32[]{:S(2)}) copy-start(f32[128,4,6]{0,2,1:T(8,128)S(1)} %get-tuple-element.105) | copy-start | bytes 36868
  27.1 60.8 %copy-start.76 = (f32[128,4,6]{0,2,1:T(8,128)}, f32[128,4,6]{0,2,1:T(8,128)S(1)}, u32[]{:S(2)}) copy-start(f32[128,4,6]{0,2,1:T(8,128)S(1)} %get-tuple-element.106) | copy-start | bytes 36868
  27.1 73.1 %copy-start.62 = (f32[128,4,12]{0,2,1:T(8,128)}, f32[128,4,12]{0,2,1:T(8,128)S(1)}, u32[]{:S(2)}) copy-start(f32[128,4,12]{0,2,1:T(8,128)S(1)} %get-tuple-element.113) | copy-start | bytes 73732
  27.2 73.1 %copy-start.64 = (f32[128,4,12]{0,2,1:T(8,128)}, f32[128,4,12]{0,2,1:T(8,128)S(1)}, u32[]{:S(2)}) copy-start(f32[128,4,12]{0,2,1:T(8,128)S(1)} %get-tuple-element.114) | copy-start | bytes 73732
  27.5 52.4 %copy-start.24 = (f32[128,4,1006]{0,2,1:T(8,128)}, f32[128,4,1006]{0,2,1:T(8,128)S(1)}, u32[]{:S(2)}) copy-start(f32[128,4,1006]{0,2,1:T(8,128)S(1)} %get-tuple-element.123) | copy-start | bytes 6180868
  27.5 52.4 %copy-start.25 = (f32[128,4,1006]{0,2,1:T(8,128)}, f32[128,4,1006]{0,2,1:T(8,128)S(1)}, u32[]{:S(2)}) copy-start(f32[128,4,1006]{0,2,1:T(8,128)S(1)} %get-tuple-element.124) | copy-start | bytes 6180868
  28.2 72.1 %copy-start.16 = (f32[128,4,1012]{0,2,1:T(8,128)}, f32[128,4,1012]{0,2,1:T(8,128)S(1)}, u32[]{:S(2)}) copy-start(f32[128,4,1012]{0,2,1:T(8,128)S(1)} %get-tuple-element.115) | copy-start | bytes 6217732
  28.2 72.1 %copy-start.18 = (f32[128,4,1012]{0,2,1:T(8,128)}, f32[128,4,1012]{0,2,1:T(8,128)S(1)}, u32[]{:S(2)}) copy-start(f32[128,4,1012]{0,2,1:T(8,128)S(1)} %get-tuple-element.116) | copy-start | bytes 6217732
  29.4 50.4 %copy-start.88 = (f32[128]{0:T(128)}, f32[128]{0:T(128)S(1)}, u32[]{:S(2)}) copy-start(f32[128]{0:T(128)S(1)} %get-tuple-element.128) | copy-start | bytes 1540
  29.4 50.4 %copy-start.89 = (f32[128]{0:T(128)}, f32[128]{0:T(128)S(1)}, u32[]{:S(2)}) copy-start(f32[128]{0:T(128)S(1)} %get-tuple-element.129) | copy-start | bytes 1540
  29.4 50.4 %copy-start.90 = (f32[128]{0:T(128)}, f32[128]{0:T(128)S(1)}, u32[]{:S(2)}) copy-start(f32[128]{0:T(128)S(1)} %get-tuple-element.130) | copy-start | bytes 1540
  29.5 50.4 %copy-start.91 = (f32[128]{0:T(128)}, f32[128]{0:T(128)S(1)}, u32[]{:S(2)}) copy-start(f32[128]{0:T(128)S(1)} %get-tuple-element.131) | copy-start | bytes 1540
  29.5 50.4 %copy-start.92 = (f32[128]{0:T(128)}, f32[128]{0:T(128)S(1)}, u32[]{:S(2)}) copy-start(f32[128]{0:T(128)S(1)} %get-tuple-element.132) | copy-start | bytes 1540
  29.5 50.4 %copy-start.93 = (f32[128]{0:T(128)}, f32[128]{0:T(128)S(1)}, u32[]{:S(2)}) copy-start(f32[128]{0:T(128)S(1)} %get-tuple-element.133) | copy-start | bytes 1540
  29.5 50.4 %copy-start.94 = (f32[128]{0:T(128)}, f32[128]{0:T(128)S(1)}, u32[]{:S(2)}) copy-start(f32[128]{0:T(128)S(1)} %get-tuple-element.134) | copy-start | bytes 1540
  29.5 50.4 %copy-start.95 = (f32[128]{0:T(128)}, f32[128]{0:T(128)S(1)}, u32[]{:S(2)}) copy-start(f32[128]{0:T(128)S(1)} %get-tuple-element.135) | copy-start | bytes 1540
  29.5 50.4 %copy-start.96 = (f32[128]{0:T(128)}, f32[128]{0:T(128)S(1)}, u32[]{:S(2)}) copy-start(f32[128]{0:T(128)S(1)} %get-tuple-element.136) | copy-start | bytes 1540
  29.5 58.4 %copy-start.86 = (f32[128]{0:T(128)}, f32[128]{0:T(128)S(1)}, u32[]{:S(2)}) copy-start(f32[128]{0:T(128)S(1)} %get-tuple-element.127) | copy-start | bytes 1540
  30.9 57.0 %copy-start.4 = (f32[128,4,1018]{0,2,1:T(8,128)}, f32[128,4,1018]{0,2,1:T(8,128)S(1)}, u32[]{:S(2)}) copy-start(f32[128,4,1018]{0,2,1:T(8,128)S(1)} %get-tuple-element.107) | copy-start | bytes 6254596
  30.9 57.0 %copy-start.6 = (f32[128,4,1018]{0,2,1:T(8,128)}, f32[128,4,1018]{0,2,1:T(8,128)S(1)}, u32[]{:S(2)}) copy-start(f32[128,4,1018]{0,2,1:T(8,128)S(1)} %get-tuple-element.108) | copy-start | bytes 6254596
  30.9 26.2 %copy-start.32 = (bf16[128,2,1024]{0,2,1:T(8,128)(2,1)}, bf16[128,2,1024]{0,2,1:T(8,128)(2,1)S(1)}, u32[]{:S(2)}) copy-start(bf16[128,2,1024]{0,2,1:T(8,128)(2,1)S(1)} %collective-permute-done.6) | copy-start | bytes 1572868
  30.9 29.8 %collective-permute-start.9 = (bf16[128,2,1024]{0,2,1:T(8,128)(2,1)}, bf16[128,2,1024]{0,2,1:T(8,128)(2,1)S(1)}, u32[]{:S(2)}, u32[]{:S(2)}) collective-permute-start(bf16[128,2,1024]{0,2,1:T(8,128)(2,1)} %get-tuple-element.126), channel_id=1, source_target_pairs={{10,0},{12,2},{14,4},{16,6},{18,8},{20,10},{22,12},{24,14},{26,16}... | collective-permute-start | bytes 1572872 | tf_op jit(solution)/shard_map/ppermute | solution.py:17
  52.6 27.3 %copy-start.35 = (bf16[128,2,1024]{0,2,1:T(8,128)(2,1)}, bf16[128,2,1024]{0,2,1:T(8,128)(2,1)S(1)}, u32[]{:S(2)}) copy-start(bf16[128,2,1024]{0,2,1:T(8,128)(2,1)S(1)} %collective-permute-done.7) | copy-start | bytes 1572868
  52.7 22.6 %collective-permute-start.3 = (bf16[128,2,1024]{0,2,1:T(8,128)(2,1)}, bf16[128,2,1024]{0,2,1:T(8,128)(2,1)S(1)}, u32[]{:S(2)}, u32[]{:S(2)}) collective-permute-start(bf16[128,2,1024]{0,2,1:T(8,128)(2,1)} %get-tuple-element.126), channel_id=1, source_target_pairs={{4,0},{6,2},{8,4},{10,6},{12,8},{14,10},{16,12},{18,14},{20,16},{2... | collective-permute-start | bytes 1572872 | tf_op jit(solution)/shard_map/ppermute | solution.py:17
  54.7 25.2 %copy-start.58 = (f32[128,4,18]{0,2,1:T(8,128)}, f32[128,4,18]{0,2,1:T(8,128)S(1)}, u32[]{:S(2)}) copy-start(f32[128,4,18]{0,2,1:T(8,128)S(1)} %get-tuple-element.85) | copy-start | bytes 110596
  54.7 25.2 %copy-start.60 = (f32[128,4,18]{0,2,1:T(8,128)}, f32[128,4,18]{0,2,1:T(8,128)S(1)}, u32[]{:S(2)}) copy-start(f32[128,4,18]{0,2,1:T(8,128)S(1)} %get-tuple-element.86) | copy-start | bytes 110596
  57.1 19.9 %collective-permute-start.1 = (bf16[128,2,1024]{0,2,1:T(8,128)(2,1)}, bf16[128,2,1024]{0,2,1:T(8,128)(2,1)S(1)}, u32[]{:S(2)}, u32[]{:S(2)}) collective-permute-start(bf16[128,2,1024]{0,2,1:T(8,128)(2,1)} %get-tuple-element.126), channel_id=1, source_target_pairs={{0,2},{2,4},{4,6},{6,8},{8,10},{10,12},{12,14},{14,16},{16,18},{18... | collective-permute-start | bytes 1572872 | tf_op jit(solution)/shard_map/ppermute | solution.py:17
  60.7 33.1 %collective-permute-start.5 = (bf16[128,4,1024]{0,2,1:T(8,128)(2,1)S(1)}, bf16[128,4,1024]{0,2,1:T(8,128)(2,1)S(1)}, u32[]{:S(2)}, u32[]{:S(2)}) collective-permute-start(bf16[128,4,1024]{0,2,1:T(8,128)(2,1)S(1)} %copy.35), channel_id=1, source_target_pairs={{6,0},{8,2},{10,4},{12,6},{14,8},{16,10},{18,12},{20,14},{22,16},{... | collective-permute-start | bytes 3145736 | tf_op jit(solution)/shard_map/ppermute | solution.py:17
  65.0 32.8 %collective-permute-start.4 = (bf16[128,4,1024]{0,2,1:T(8,128)(2,1)S(1)}, bf16[128,4,1024]{0,2,1:T(8,128)(2,1)S(1)}, u32[]{:S(2)}, u32[]{:S(2)}) collective-permute-start(bf16[128,4,1024]{0,2,1:T(8,128)(2,1)S(1)} %copy.35), channel_id=1, source_target_pairs={{0,6},{2,8},{4,10},{6,12},{8,14},{10,16},{12,18},{14,20},{16,22},{... | collective-permute-start | bytes 3145736 | tf_op jit(solution)/shard_map/ppermute | solution.py:17
  142.7 194.8 %reduce-scatter.4.cloned.1.call-start = ((), (), s32[]{:S(2)}) async-start(), calls=%async_computation.3 | async-start | bytes 3145728
  153.8 116.9 %collective-permute-start.18 = (bf16[128,2,1024]{0,2,1:T(8,128)(2,1)}, bf16[128,2,1024]{0,2,1:T(8,128)(2,1)S(1)}, u32[]{:S(2)}, u32[]{:S(2)}) collective-permute-start(bf16[128,2,1024]{0,2,1:T(8,128)(2,1)} %get-tuple-element.93), channel_id=1, source_target_pairs={{0,10},{2,12},{4,14},{6,16},{8,18},{10,20},{12,22},{14,24},{16,26}... | collective-permute-start | bytes 1572872 | tf_op jit(solution)/shard_map/ppermute | solution.py:17
  166.0 94.9 %collective-permute-start.16 = (bf16[128,2,1024]{0,2,1:T(8,128)(2,1)}, bf16[128,2,1024]{0,2,1:T(8,128)(2,1)S(1)}, u32[]{:S(2)}, u32[]{:S(2)}) collective-permute-start(bf16[128,2,1024]{0,2,1:T(8,128)(2,1)} %get-tuple-element.93), channel_id=1, source_target_pairs={{8,0},{10,2},{12,4},{14,6},{16,8},{18,10},{20,12},{22,14},{24,16},... | collective-permute-start | bytes 1572872 | tf_op jit(solution)/shard_map/ppermute | solution.py:17
  167.3 105.4 %collective-permute-start.19 = (bf16[128,2,1024]{0,2,1:T(8,128)(2,1)}, bf16[128,2,1024]{0,2,1:T(8,128)(2,1)S(1)}, u32[]{:S(2)}, u32[]{:S(2)}) collective-permute-start(bf16[128,2,1024]{0,2,1:T(8,128)(2,1)} %get-tuple-element.94), channel_id=1, source_target_pairs={{0,8},{2,10},{4,12},{6,14},{8,16},{10,18},{12,20},{14,22},{16,24},... | collective-permute-start | bytes 1572872 | tf_op jit(solution)/shard_map/ppermute | solution.py:17
  171.3 92.4 %collective-permute-start.17 = (bf16[128,2,1024]{0,2,1:T(8,128)(2,1)}, bf16[128,2,1024]{0,2,1:T(8,128)(2,1)S(1)}, u32[]{:S(2)}, u32[]{:S(2)}) collective-permute-start(bf16[128,2,1024]{0,2,1:T(8,128)(2,1)} %get-tuple-element.94), channel_id=1, source_target_pairs={{10,0},{12,2},{14,4},{16,6},{18,8},{20,10},{22,12},{24,14},{26,16}... | collective-permute-start | bytes 1572872 | tf_op jit(solution)/shard_map/ppermute | solution.py:17
  180.7 106.9 %collective-permute-start.12 = (bf16[128,2,1024]{0,2,1:T(8,128)(2,1)}, bf16[128,2,1024]{0,2,1:T(8,128)(2,1)}, u32[]{:S(2)}, u32[]{:S(2)}) collective-permute-start(bf16[128,2,1024]{0,2,1:T(8,128)(2,1)} %get-tuple-element.103), channel_id=1, source_target_pairs={{0,4},{2,6},{4,8},{6,10},{8,12},{10,14},{12,16},{14,18},{16,20},{1... | collective-permute-start | bytes 1572872 | tf_op jit(solution)/shard_map/ppermute | solution.py:17
  260.9 17.1 %collective-permute-start.10 = (bf16[128,2,1024]{0,2,1:T(8,128)(2,1)}, bf16[128,2,1024]{0,2,1:T(8,128)(2,1)S(1)}, u32[]{:S(2)}, u32[]{:S(2)}) collective-permute-start(bf16[128,2,1024]{0,2,1:T(8,128)(2,1)} %get-tuple-element.103), channel_id=1, source_target_pairs={{2,0},{4,2},{6,4},{8,6},{10,8},{12,10},{14,12},{16,14},{18,16},{20... | collective-permute-start | bytes 1572872 | tf_op jit(solution)/shard_map/ppermute | solution.py:17
  263.7 23.9 %collective-permute-start.13 = (bf16[128,2,1024]{0,2,1:T(8,128)(2,1)}, bf16[128,2,1024]{0,2,1:T(8,128)(2,1)S(1)}, u32[]{:S(2)}, u32[]{:S(2)}) collective-permute-start(bf16[128,2,1024]{0,2,1:T(8,128)(2,1)} %get-tuple-element.104), channel_id=1, source_target_pairs={{0,2},{2,4},{4,6},{6,8},{8,10},{10,12},{12,14},{14,16},{16,18},{18... | collective-permute-start | bytes 1572872 | tf_op jit(solution)/shard_map/ppermute | solution.py:17
  270.7 16.7 %collective-permute-start.11 = (bf16[128,2,1024]{0,2,1:T(8,128)(2,1)}, bf16[128,2,1024]{0,2,1:T(8,128)(2,1)S(1)}, u32[]{:S(2)}, u32[]{:S(2)}) collective-permute-start(bf16[128,2,1024]{0,2,1:T(8,128)(2,1)} %get-tuple-element.104), channel_id=1, source_target_pairs={{4,0},{6,2},{8,4},{10,6},{12,8},{14,10},{16,12},{18,14},{20,16},{2... | collective-permute-start | bytes 1572872 | tf_op jit(solution)/shard_map/ppermute | solution.py:17
  272.7 39.9 %collective-permute-start.15 = (bf16[128,4,1024]{0,2,1:T(8,128)(2,1)S(1)}, bf16[128,4,1024]{0,2,1:T(8,128)(2,1)S(1)}, u32[]{:S(2)}, u32[]{:S(2)}) collective-permute-start(bf16[128,4,1024]{0,2,1:T(8,128)(2,1)S(1)} %copy-done.54), channel_id=1, source_target_pairs={{0,6},{2,8},{4,10},{6,12},{8,14},{10,16},{12,18},{14,20},{16,22},{... | collective-permute-start | bytes 3145736 | tf_op jit(solution)/shard_map/ppermute | solution.py:17
  278.0 34.6 %collective-permute-start.14 = (bf16[128,4,1024]{0,2,1:T(8,128)(2,1)S(1)}, bf16[128,4,1024]{0,2,1:T(8,128)(2,1)S(1)}, u32[]{:S(2)}, u32[]{:S(2)}) collective-permute-start(bf16[128,4,1024]{0,2,1:T(8,128)(2,1)S(1)} %copy-done.54), channel_id=1, source_target_pairs={{6,0},{8,2},{10,4},{12,6},{14,8},{16,10},{18,12},{20,14},{22,16},{... | collective-permute-start | bytes 3145736 | tf_op jit(solution)/shard_map/ppermute | solution.py:17
  (81 other events, 390.8 us)
Sparse Core Ops, SparseCore 0:
  23.9 33.2 all-gather.1
  142.8 114.6 all-reduce.1
  259.7 32.5 reduce-scatter.3
